TPU v7x, 256 devices: a whole 4x4x8 slice. The times are simulated.
256 devices in a mesh: dp: 16 (over y_hi, z), seq: 16 (over x, y_lo, core).
Axes of the slice: x: 4, y: 4 (y_hi: 2, y_lo: 2; y = y_hi * 2 + y_lo), z: 8, core: 2. Of those that a mesh axis runs over, the one named last changes fastest.
Arguments:
- queries: bfloat16 [16, 2048, 2048], P('dp', 'seq'), may hold values from -6 to 6
- key_states: bfloat16 [16, 2048, 2048], P('dp', 'seq'), may hold values from -6 to 6
- value_states: bfloat16 [16, 2048, 2048], P('dp', 'seq'), may hold values from -6 to 6
- cotangent: bfloat16 [16, 2048, 2048], P('dp', 'seq'), may hold values from -6 to 6
- filter_taps: float32 [7, 2048], replicated, may hold values from -3 to 3
Outputs:
- conv_output: bfloat16 [16, 2048, 2048], P('dp', 'seq')
- grad_queries: bfloat16 [16, 2048, 2048], P('dp', 'seq')
- grad_keys: bfloat16 [16, 2048, 2048], P('dp', 'seq')
- grad_values: bfloat16 [16, 2048, 2048], P('dp', 'seq')
- filter_gradient: float32 [7, 2048], replicated
All inputs are finite; a program needn't handle non-finite values.
Results may differ from a plain program's by a relative error of at most 0.015.
Values may be sent and summed in bfloat16 or wider, within the bound.
No kernel may reach another device: no remote copies, remote signals or barrier semaphores. Data moves between devices by JAX's collectives and lax.ppermute only.
A program may use at most 128 MiB of HBM per device.

v0:
```python
import math
import jax
import jax.numpy as jnp
from jax import lax
from jax.sharding import PartitionSpec as P

HD = 128
TAPS = 7


def padded(value, sides, width):
    for axis, dim in sides:
        peers, length = (lax.axis_size(axis), value.shape[dim])
        up = [(i, (i + 1) % peers) for i in range(peers)]
        down = [(j, i) for i, j in up]
        last = lax.slice_in_dim(value, length - width, length, axis=dim)
        leading = lax.slice_in_dim(value, 0, width, axis=dim)
        before = lax.ppermute(last, axis, up)
        after = lax.ppermute(leading, axis, down)
        value = jnp.concatenate([before, value, after], axis=dim)
    return value


def on_device(queries, key_states, value_states, cotangent, filter_taps):
    tok_rows = queries.shape[1]
    channels = queries.shape[2]
    sequence_shards = lax.axis_size("seq")
    seq_total = tok_rows * sequence_shards
    head_count = channels // HD
    group_heads = math.gcd(head_count, 4)
    group_width = group_heads * HD
    group_count = head_count // group_heads
    score_scale = HD ** (-0.5)
    half_width = (TAPS - 1) // 2
    local_q = queries[0]
    local_k = key_states[0]
    local_v = value_states[0]
    local_g = cotangent[0]
    grad_pad = padded(local_g, (("seq", 0),), half_width)
    grad_sum = jnp.zeros((tok_rows, channels), jnp.float32)
    for tap_index in range(TAPS):
        start_row = 2 * half_width - tap_index
        grad_sum = grad_sum + filter_taps[tap_index] * grad_pad[
            start_row : start_row + tok_rows
        ].astype(jnp.float32)
    grad_attn = grad_sum.astype(jnp.bfloat16)
    key_all, value_all = (
        lax.all_gather(local_k, "seq", axis=0, tiled=True),
        lax.all_gather(local_v, "seq", axis=0, tiled=True),
    )
    device_index = lax.axis_index("seq")
    query_pos = device_index * tok_rows + jnp.arange(tok_rows, dtype=jnp.int32)
    key_pos = jnp.arange(seq_total, dtype=jnp.int32)
    visible = query_pos[:, None] >= key_pos[None, :]

    def columns(matrix, group_index, count):
        picked = lax.dynamic_slice_in_dim(matrix, group_index * group_width, group_width, 1)
        return picked.reshape(count, group_heads, HD)

    def forward_group(group_index):
        q_part = columns(local_q, group_index, tok_rows)
        k_part = columns(key_all, group_index, seq_total)
        v_part = columns(value_all, group_index, seq_total)
        delta_portion = columns(grad_attn, group_index, tok_rows)
        scores = (
            jnp.einsum("thd,uhd->htu", q_part, k_part, preferred_element_type=jnp.float32)
            * score_scale
        )
        row_top = jnp.max(jnp.where(visible, scores, -jnp.inf), -1, keepdims=True)
        raw = jnp.where(visible, jnp.exp(scores - row_top), 0.0)
        row_total = jnp.sum(raw, -1, keepdims=True)
        probs = raw / row_total
        probs_low = probs.astype(jnp.bfloat16)
        attended = jnp.einsum("htu,uhd->thd", probs_low, v_part, preferred_element_type=jnp.float32)
        attended = attended.astype(jnp.bfloat16).reshape(tok_rows, group_width)
        dprob = jnp.einsum(
            "thd,uhd->htu", delta_portion, v_part, preferred_element_type=jnp.float32
        )
        row_delta = jnp.sum(probs * dprob, -1, keepdims=True)
        dscore = (probs * (dprob - row_delta) * score_scale).astype(jnp.bfloat16)
        grad_q = jnp.einsum("htu,uhd->thd", dscore, k_part, preferred_element_type=jnp.float32)
        grad_q = grad_q.astype(jnp.bfloat16).reshape(tok_rows, group_width)
        key_term = jnp.einsum("htu,thd->uhd", dscore, q_part, preferred_element_type=jnp.float32)
        value_term = jnp.einsum(
            "htu,thd->uhd", probs_low, delta_portion, preferred_element_type=jnp.float32
        )
        return (
            attended,
            grad_q,
            key_term.reshape(seq_total, group_width),
            value_term.reshape(seq_total, group_width),
        )

    group_ids = jnp.arange(group_count, dtype=jnp.int32)
    attended, grad_q, key_term, value_term = lax.map(forward_group, group_ids)
    key_share, value_share = (
        lax.psum_scatter(
            key_term.astype(jnp.bfloat16), "seq", scatter_dimension=1, tiled=True
        ).astype(jnp.float32),
        lax.psum_scatter(
            value_term.astype(jnp.bfloat16), "seq", scatter_dimension=1, tiled=True
        ).astype(jnp.float32),
    )
    grad_keys = key_share.transpose(1, 0, 2).reshape(tok_rows, channels).astype(jnp.bfloat16)
    grad_values = value_share.transpose(1, 0, 2).reshape(tok_rows, channels).astype(jnp.bfloat16)
    attn_out = attended.transpose(1, 0, 2).reshape(tok_rows, channels)
    grad_queries = grad_q.transpose(1, 0, 2).reshape(tok_rows, channels)
    out_pad = padded(attn_out, (("seq", 0),), half_width)
    conv_sum = jnp.zeros((tok_rows, channels), jnp.float32)
    filter_rows = []
    local_gf = local_g.astype(jnp.float32)
    for tap_index in range(TAPS):
        moved = out_pad[tap_index : tap_index + tok_rows].astype(jnp.float32)
        conv_sum = conv_sum + filter_taps[tap_index] * moved
        filter_rows.append(jnp.sum(moved * local_gf, 0))
    filter_gradient = lax.psum(jnp.stack(filter_rows, 0), ("dp", "seq"))
    conv_output = conv_sum.astype(jnp.bfloat16)
    return (
        conv_output[None],
        grad_queries[None],
        grad_keys[None],
        grad_values[None],
        filter_gradient,
    )


def solution(mesh):
    in_specs = (
        P("dp", "seq", None),
        P("dp", "seq", None),
        P("dp", "seq", None),
        P("dp", "seq", None),
        P(),
    )
    out_specs = (
        P("dp", "seq", None),
        P("dp", "seq", None),
        P("dp", "seq", None),
        P("dp", "seq", None),
        P(),
    )
    return jax.shard_map(
        on_device, mesh=mesh, in_specs=in_specs, out_specs=out_specs, check_vma=False
    )
```

profile of v0, /device:TPU:1, one launch (start us, length us, event | category | flops | bytes accessed | tf_op | source)
XLA Modules:
  0.0 557.8 jit_solution(18201332075401801703)
XLA Ops:
  20.9 57.9 %all-gather.5.cloned.1.call-done = bf16[1,2048,2048]{1,2,0:T(8,128)(2,1)} async-done(((bf16[1,128,2048]{1,2,0:T(8,128)(2,1)}), bf16[1,2048,2048]{1,2,0:T(8,128)(2,1)}) %all-gather.5.cloned.1.call-update) | async-done | bytes 8388624 | tf_op jit(solution)/shard_map/all_gather | solution.py:49
  78.7 65.4 %all-gather.7.cloned.1.call-done = bf16[1,2048,2048]{1,2,0:T(8,128)(2,1)} async-done(((bf16[1,128,2048]{1,2,0:T(8,128)(2,1)}), bf16[1,2048,2048]{1,2,0:T(8,128)(2,1)}) %all-gather.7.cloned.1.call-update) | async-done | bytes 8388624 | tf_op jit(solution)/shard_map/all_gather | solution.py:48
  144.2 177.4 %while.17 = (s32[]{:T(128)}, bf16[4,128,512]{1,2,0:T(8,128)(2,1)S(1)}, bf16[4,128,512]{1,2,0:T(8,128)(2,1)}, bf16[4,2048,512]{1,2,0:T(8,128)(2,1)}, bf16[4,2048,...) while((s32[]{:T(128)}, ...), condition=%wide.region_4.5_spmd.clone, body=%wide.region_0.4_spmd.clone.sunk | while | flops 1904614400 | bytes 82324224 | solution.py:95
  145.5 3.2 constant_dynamic-slice_fusion.8
  155.4 6.5 %fusion.111 = (f32[4,128]{1,0:T(4,128)S(1)}, f32[4,128,2048]{2,1,0:T(8,128)}) fusion(pred[128,2048]{1,0:T(8,128)(4,1)S(1)} %iota_compare_fusion.2, bf16[128,4,128]{0,2,1:T(8,128)(2,1)S(1)} %bitcast.143, bf16[2048,4,128]{0,2,1:T(8,128)(2,1)} %bitcast.125), kind=kOutput, calls=%fused_computation.95.clone.1 | convolution fusion | flops 543164416 | bytes 6686720 | tf_op jit(solution)/shard_map/while/body/eval_jaxpr/sub | solution.py:70
  161.9 8.5 %fusion.112 = bf16[4,128,128]{2,1,0:T(8,128)(2,1)S(1)} fusion(bf16[2048,4,128]{0,2,1:T(8,128)(2,1)} %bitcast.126, f32[4,128,2048]{2,1,0:T(8,128)} %fusion.110, f32[4,128,2048]{2,1,0:T(8,128)} %get-tuple-element.242, f32[4,128]{1,0:T(4,128)S(1)} %get-tuple-element.243), kind=kOutput, calls=%fused_computation.18.clone.1 | convolution fusion | flops 275843584 | bytes 10618880 | tf_op jit(solution)/shard_map/while/body/eval_jaxpr/htu,uhd->thd/dot_general | solution.py:81
  170.5 3.1 convolution_convert_fusion.2
  175.1 9.5 %fusion.114 = bf16[4,128,2048]{2,1,0:T(8,128)(2,1)} fusion(bf16[128,4,128]{0,2,1:T(8,128)(2,1)S(1)} %bitcast.144, f32[4,128,2048]{2,1,0:T(8,128)} %fusion.110, f32[4,128,2048]{2,1,0:T(8,128)} %get-tuple-element.242, f32[4,128]{1,0:T(4,128)S(1)} %get-tuple-element.243), kind=kOutput, calls=%fused_computation.10.clone.1 | convolution fusion | flops 275778048 | bytes 10618880 | tf_op jit(solution)/shard_map/while/body/eval_jaxpr/htu,thd->uhd/dot_general | solution.py:83
  184.6 4.0 constant_dynamic-update-slice_fusion.7
  189.8 3.2 constant_dynamic-slice_fusion.8
  199.7 6.5 %fusion.111 = (f32[4,128]{1,0:T(4,128)S(1)}, f32[4,128,2048]{2,1,0:T(8,128)}) fusion(pred[128,2048]{1,0:T(8,128)(4,1)S(1)} %iota_compare_fusion.2, bf16[128,4,128]{0,2,1:T(8,128)(2,1)S(1)} %bitcast.143, bf16[2048,4,128]{0,2,1:T(8,128)(2,1)} %bitcast.125), kind=kOutput, calls=%fused_computation.95.clone.1 | convolution fusion | flops 543164416 | bytes 6686720 | tf_op jit(solution)/shard_map/while/body/eval_jaxpr/sub | solution.py:70
  206.3 8.5 %fusion.112 = bf16[4,128,128]{2,1,0:T(8,128)(2,1)S(1)} fusion(bf16[2048,4,128]{0,2,1:T(8,128)(2,1)} %bitcast.126, f32[4,128,2048]{2,1,0:T(8,128)} %fusion.110, f32[4,128,2048]{2,1,0:T(8,128)} %get-tuple-element.242, f32[4,128]{1,0:T(4,128)S(1)} %get-tuple-element.243), kind=kOutput, calls=%fused_computation.18.clone.1 | convolution fusion | flops 275843584 | bytes 10618880 | tf_op jit(solution)/shard_map/while/body/eval_jaxpr/htu,uhd->thd/dot_general | solution.py:81
  219.4 9.5 %fusion.114 = bf16[4,128,2048]{2,1,0:T(8,128)(2,1)} fusion(bf16[128,4,128]{0,2,1:T(8,128)(2,1)S(1)} %bitcast.144, f32[4,128,2048]{2,1,0:T(8,128)} %fusion.110, f32[4,128,2048]{2,1,0:T(8,128)} %get-tuple-element.242, f32[4,128]{1,0:T(4,128)S(1)} %get-tuple-element.243), kind=kOutput, calls=%fused_computation.10.clone.1 | convolution fusion | flops 275778048 | bytes 10618880 | tf_op jit(solution)/shard_map/while/body/eval_jaxpr/htu,thd->uhd/dot_general | solution.py:83
  228.9 4.0 constant_dynamic-update-slice_fusion.7
  234.2 3.2 constant_dynamic-slice_fusion.8
  244.1 6.5 %fusion.111 = (f32[4,128]{1,0:T(4,128)S(1)}, f32[4,128,2048]{2,1,0:T(8,128)}) fusion(pred[128,2048]{1,0:T(8,128)(4,1)S(1)} %iota_compare_fusion.2, bf16[128,4,128]{0,2,1:T(8,128)(2,1)S(1)} %bitcast.143, bf16[2048,4,128]{0,2,1:T(8,128)(2,1)} %bitcast.125), kind=kOutput, calls=%fused_computation.95.clone.1 | convolution fusion | flops 543164416 | bytes 6686720 | tf_op jit(solution)/shard_map/while/body/eval_jaxpr/sub | solution.py:70
  250.6 8.5 %fusion.112 = bf16[4,128,128]{2,1,0:T(8,128)(2,1)S(1)} fusion(bf16[2048,4,128]{0,2,1:T(8,128)(2,1)} %bitcast.126, f32[4,128,2048]{2,1,0:T(8,128)} %fusion.110, f32[4,128,2048]{2,1,0:T(8,128)} %get-tuple-element.242, f32[4,128]{1,0:T(4,128)S(1)} %get-tuple-element.243), kind=kOutput, calls=%fused_computation.18.clone.1 | convolution fusion | flops 275843584 | bytes 10618880 | tf_op jit(solution)/shard_map/while/body/eval_jaxpr/htu,uhd->thd/dot_general | solution.py:81
  259.2 3.1 convolution_convert_fusion.2
  263.8 9.5 %fusion.114 = bf16[4,128,2048]{2,1,0:T(8,128)(2,1)} fusion(bf16[128,4,128]{0,2,1:T(8,128)(2,1)S(1)} %bitcast.144, f32[4,128,2048]{2,1,0:T(8,128)} %fusion.110, f32[4,128,2048]{2,1,0:T(8,128)} %get-tuple-element.242, f32[4,128]{1,0:T(4,128)S(1)} %get-tuple-element.243), kind=kOutput, calls=%fused_computation.10.clone.1 | convolution fusion | flops 275778048 | bytes 10618880 | tf_op jit(solution)/shard_map/while/body/eval_jaxpr/htu,thd->uhd/dot_general | solution.py:83
  273.3 4.0 constant_dynamic-update-slice_fusion.7
  278.5 3.2 constant_dynamic-slice_fusion.8
  288.4 6.5 %fusion.111 = (f32[4,128]{1,0:T(4,128)S(1)}, f32[4,128,2048]{2,1,0:T(8,128)}) fusion(pred[128,2048]{1,0:T(8,128)(4,1)S(1)} %iota_compare_fusion.2, bf16[128,4,128]{0,2,1:T(8,128)(2,1)S(1)} %bitcast.143, bf16[2048,4,128]{0,2,1:T(8,128)(2,1)} %bitcast.125), kind=kOutput, calls=%fused_computation.95.clone.1 | convolution fusion | flops 543164416 | bytes 6686720 | tf_op jit(solution)/shard_map/while/body/eval_jaxpr/sub | solution.py:70
  294.9 8.5 %fusion.112 = bf16[4,128,128]{2,1,0:T(8,128)(2,1)S(1)} fusion(bf16[2048,4,128]{0,2,1:T(8,128)(2,1)} %bitcast.126, f32[4,128,2048]{2,1,0:T(8,128)} %fusion.110, f32[4,128,2048]{2,1,0:T(8,128)} %get-tuple-element.242, f32[4,128]{1,0:T(4,128)S(1)} %get-tuple-element.243), kind=kOutput, calls=%fused_computation.18.clone.1 | convolution fusion | flops 275843584 | bytes 10618880 | tf_op jit(solution)/shard_map/while/body/eval_jaxpr/htu,uhd->thd/dot_general | solution.py:81
  303.5 3.1 convolution_convert_fusion.2
  308.1 9.5 %fusion.114 = bf16[4,128,2048]{2,1,0:T(8,128)(2,1)} fusion(bf16[128,4,128]{0,2,1:T(8,128)(2,1)S(1)} %bitcast.144, f32[4,128,2048]{2,1,0:T(8,128)} %fusion.110, f32[4,128,2048]{2,1,0:T(8,128)} %get-tuple-element.242, f32[4,128]{1,0:T(4,128)S(1)} %get-tuple-element.243), kind=kOutput, calls=%fused_computation.10.clone.1 | convolution fusion | flops 275778048 | bytes 10618880 | tf_op jit(solution)/shard_map/while/body/eval_jaxpr/htu,thd->uhd/dot_general | solution.py:83
  317.6 4.0 constant_dynamic-update-slice_fusion.7
  321.6 14.6 %copy.60 = bf16[4,2048,512]{2,0,1:T(4,128)(2,1)} copy(bf16[4,2048,512]{1,2,0:T(8,128)(2,1)} %get-tuple-element.67) | data formatting | bytes 16777216
  336.2 10.2 %copy.65 = bf16[256,8,4,512]{3,1,2,0:T(8,128)(2,1)} copy(bf16[256,8,4,512]{3,2,1,0:T(4,128)(2,1)} %bitcast.131) | data formatting | bytes 16777216
  346.5 14.6 %copy.62 = bf16[4,2048,512]{2,0,1:T(4,128)(2,1)} copy(bf16[4,2048,512]{1,2,0:T(8,128)(2,1)} %get-tuple-element.68) | data formatting | bytes 16777216
  361.0 10.2 %copy.66 = bf16[256,8,4,512]{3,1,2,0:T(8,128)(2,1)} copy(bf16[256,8,4,512]{3,2,1,0:T(4,128)(2,1)} %bitcast.132) | data formatting | bytes 16777216
  379.1 78.2 %psum.7 = f32[7,2048]{1,0:T(8,128)} all-reduce(f32[7,2048]{1,0:T(8,128)S(1)} %stack.31), channel_id=1, replica_groups=mesh['dp'=16,'seq'=16] {'dp','seq'}, use_global_device_ids=true, to_apply=%region_14.15 | all-reduce | flops 14336 | bytes 114688 | tf_op jit(solution)/shard_map/psum | solution.py:116
  462.0 86.5 %reduce-scatter.9.cloned.1.call-done = bf16[128,2048]{1,0:T(8,128)(2,1)} async-done(((bf16[2048,2048]{1,0:T(8,128)(2,1)}), bf16[128,2048]{1,0:T(8,128)(2,1)}) %reduce-scatter.9.cloned.1.call-update) | async-done | bytes 524304
  (123 shorter events, 66.9 us)
Async XLA Ops:
  7.2 11.9 %copy-start = (bf16[1,128,2048]{2,1,0:T(8,128)(2,1)S(1)}, bf16[1,128,2048]{2,1,0:T(8,128)(2,1)}, u32[]{:S(2)}) copy-start(bf16[1,128,2048]{2,1,0:T(8,128)(2,1)} %param.10) | copy-start | bytes 1572868
  7.2 71.6 %all-gather.5.cloned.1.call-start = ((), (), s32[]{:S(2)}) async-start(), calls=%async_computation.2 | async-start | bytes 8912896 | tf_op jit(solution)/shard_map/all_gather | solution.py:49
  9.3 134.8 %all-gather.7.cloned.1.call-start = ((), (), s32[]{:S(2)}) async-start(), calls=%async_computation.3 | async-start | bytes 8912896 | tf_op jit(solution)/shard_map/all_gather | solution.py:48
  11.5 447.6 %reduce-scatter.7.cloned.1.call-start = ((), (), s32[]{:S(2)}) async-start(), calls=%async_computation.4 | async-start | bytes 8912896
  12.3 6.8 %collective-permute-start.1 = (bf16[3,2048]{1,0:T(4,128)(2,1)S(1)}, bf16[3,2048]{1,0:T(4,128)(2,1)S(1)}, u32[]{:S(2)}, u32[]{:S(2)}) collective-permute-start(bf16[3,2048]{1,0:T(4,128)(2,1)S(1)} %get-tuple-element.161), channel_id=1, source_target_pairs={{0,1},{1,2},{2,3},{3,4},{4,5},{5,6},{6,7},{7,8},{8,9},{9,10},{10,1... | collective-permute-start | bytes 36872 | tf_op jit(solution)/shard_map/ppermute | solution.py:18
  15.1 4.0 collective-permute-start
  16.9 127.2 %copy-start.2 = (f32[1,2048]{1,0:T(1,128)}, f32[1,2048]{1,0:T(1,128)S(1)}, u32[]{:S(2)}) copy-start(f32[1,2048]{1,0:T(1,128)S(1)} %get-tuple-element.162) | copy-start | bytes 24580
  16.9 127.2 %copy-start.4 = (f32[1,2048]{1,0:T(1,128)}, f32[1,2048]{1,0:T(1,128)S(1)}, u32[]{:S(2)}) copy-start(f32[1,2048]{1,0:T(1,128)S(1)} %get-tuple-element.163) | copy-start | bytes 24580
  16.9 127.2 %copy-start.6 = (f32[1,2048]{1,0:T(1,128)}, f32[1,2048]{1,0:T(1,128)S(1)}, u32[]{:S(2)}) copy-start(f32[1,2048]{1,0:T(1,128)S(1)} %get-tuple-element.164) | copy-start | bytes 24580
  17.0 127.2 %copy-start.8 = (f32[1,2048]{1,0:T(1,128)}, f32[1,2048]{1,0:T(1,128)S(1)}, u32[]{:S(2)}) copy-start(f32[1,2048]{1,0:T(1,128)S(1)} %get-tuple-element.165) | copy-start | bytes 24580
  17.0 127.2 %copy-start.10 = (f32[1,2048]{1,0:T(1,128)}, f32[1,2048]{1,0:T(1,128)S(1)}, u32[]{:S(2)}) copy-start(f32[1,2048]{1,0:T(1,128)S(1)} %get-tuple-element.166) | copy-start | bytes 24580
  17.0 127.2 %copy-start.12 = (f32[1,2048]{1,0:T(1,128)}, f32[1,2048]{1,0:T(1,128)S(1)}, u32[]{:S(2)}) copy-start(f32[1,2048]{1,0:T(1,128)S(1)} %get-tuple-element.167) | copy-start | bytes 24580
  17.0 127.2 %copy-start.14 = (f32[1,2048]{1,0:T(1,128)}, f32[1,2048]{1,0:T(1,128)S(1)}, u32[]{:S(2)}) copy-start(f32[1,2048]{1,0:T(1,128)S(1)} %get-tuple-element.168) | copy-start | bytes 24580
  170.5 3.8 copy-start.16
  214.8 3.8 copy-start.16
  259.1 3.8 copy-start.16
  303.5 3.8 copy-start.16
  346.4 202.0 %reduce-scatter.9.cloned.1.call-start = ((), (), s32[]{:S(2)}) async-start(), calls=%async_computation.5 | async-start | bytes 8912896
  371.3 1.0 copy-start.1
  372.5 84.8 %copy-start.3 = (f32[1,2048]{1,0:T(1,128)S(1)}, f32[1,2048]{1,0:T(1,128)}, u32[]{:S(2)}) copy-start(f32[1,2048]{1,0:T(1,128)} %copy-done.2) | copy-start | bytes 24580
  372.5 84.8 %copy-start.5 = (f32[1,2048]{1,0:T(1,128)S(1)}, f32[1,2048]{1,0:T(1,128)}, u32[]{:S(2)}) copy-start(f32[1,2048]{1,0:T(1,128)} %copy-done.4) | copy-start | bytes 24580
  372.6 84.8 %copy-start.7 = (f32[1,2048]{1,0:T(1,128)S(1)}, f32[1,2048]{1,0:T(1,128)}, u32[]{:S(2)}) copy-start(f32[1,2048]{1,0:T(1,128)} %copy-done.6) | copy-start | bytes 24580
  372.6 84.7 %copy-start.9 = (f32[1,2048]{1,0:T(1,128)S(1)}, f32[1,2048]{1,0:T(1,128)}, u32[]{:S(2)}) copy-start(f32[1,2048]{1,0:T(1,128)} %copy-done.8) | copy-start | bytes 24580
  372.6 84.7 %copy-start.11 = (f32[1,2048]{1,0:T(1,128)S(1)}, f32[1,2048]{1,0:T(1,128)}, u32[]{:S(2)}) copy-start(f32[1,2048]{1,0:T(1,128)} %copy-done.10) | copy-start | bytes 24580
  372.6 84.7 %copy-start.13 = (f32[1,2048]{1,0:T(1,128)S(1)}, f32[1,2048]{1,0:T(1,128)}, u32[]{:S(2)}) copy-start(f32[1,2048]{1,0:T(1,128)} %copy-done.12) | copy-start | bytes 24580
  372.6 84.7 %copy-start.15 = (f32[1,2048]{1,0:T(1,128)S(1)}, f32[1,2048]{1,0:T(1,128)}, u32[]{:S(2)}) copy-start(f32[1,2048]{1,0:T(1,128)} %copy-done.14) | copy-start | bytes 24580
  373.0 4.9 collective-permute-start.3
  373.7 4.3 collective-permute-start.2
Sparse Core Ops, SparseCore 0:
  10.4 68.3 all-gather.4
  81.1 63.0 all-gather.6
  346.6 99.6 reduce-scatter.6
  448.7 99.6 reduce-scatter.8
where the time goes:
time: 560 us; the launch traced here: 558 us
  waiting for transfers between devices  210 us (38%)
  matrix products  125 us (22%)
  local copies, waits for them, and re-layouts  116 us (21%)
  blocking collectives  78.2 us (14%)
  between operations  14.1 us (3%)
  other arithmetic  5.7 us (1%)
  starting transfers between devices  5.66 us (1%)
    unnamed x6, waiting for transfers between devices  86.6 us
    psum x1, blocking collectives, on_device(): filter_gradient = lax.psum(jnp.stack(filter_rows, 0), ('dp', 'seq'))  78.2 us
    all_gather x1, waiting for transfers between devices, on_device(): lax.all_gather(local_k, 'seq', axis=0, tiled=True)  65.4 us
    unnamed x46, local copies, waits for them, and re-layouts  62.6 us
    all_gather x1, waiting for transfers between devices, on_device(): lax.all_gather(local_v, 'seq', axis=0, tiled=True)  57.9 us
    dot_general x4, matrix products, forward_group(): jnp.einsum('htu,thd->uhd', dscore, q_part, preferred_element_type=jnp.flo...  38 us
    dot_general x4, matrix products, forward_group(): jnp.einsum('htu,uhd->thd', dscore, k_part, preferred_element_type=jnp.flo...  34.2 us
    dynamic_slice x20, local copies, waits for them, and re-layouts, columns(): lax.dynamic_slice_in_dim(matrix, group_index * group_width, group_width, 1)  27.5 us
  transfers between devices with their start and end apart: 8, of which 3 were waited for; matrix products, arithmetic and copies ran while one was open for 7% of the time, Pallas kernels for 0%

commit v1 on v0

--- a/solution.py
+++ b/solution.py
@@ -46,7 +46,9 @@
     grad_attn = grad_sum.astype(jnp.bfloat16)
     key_all, value_all = (
         lax.all_gather(local_k, "seq", axis=0, tiled=True),
-        lax.all_gather(local_v, "seq", axis=0, tiled=True),
+        jnp.concatenate(
+            lax.all_to_all(jnp.stack([local_v] * lax.axis_size("seq")), "seq", 0, 0), axis=0
+        ),
     )
     device_index = lax.axis_index("seq")
     query_pos = device_index * tok_rows + jnp.arange(tok_rows, dtype=jnp.int32)

time: 560 us -> 623 us (1.11)
  local copies, waits for them, and re-layouts: 116 us -> 147 us
  waiting for transfers between devices: 210 us -> 227 us
  starting transfers between devices: 5.66 us -> 19 us
    ppermute x2, waiting for transfers between devices: 0.01 us -> 78 us  [padded(): before = lax.ppermute(last, axis, up)]
    all_gather x1, waiting for transfers between devices: 65.4 us -> 1.21 us  [on_device(): lax.all_gather(local_k, 'seq', axis=0, tiled=True)]
    all_gather x1 -> x0, waiting for transfers between devices: 57.9 us -> none  [on_device(): lax.all_gather(local_v, 'seq', axis=0, tiled=True)]
    all_to_all x0 -> x1, waiting for transfers between devices: none -> 48.8 us  [on_device(): lax.all_to_all(jnp.stack([local_v] * lax.axis_size('seq')), 'seq', 0, 0)]
    dynamic_slice x20 -> x24, local copies, waits for them, and re-layouts: 27.5 us -> 44.6 us  [columns(): lax.dynamic_slice_in_dim(matrix, group_index * group_width, group_width, 1)]
    all_to_all x0 -> x1, local copies, waits for them, and re-layouts: none -> 12.3 us  [on_device(): lax.all_to_all(jnp.stack([local_v] * lax.axis_size('seq')), 'seq', 0, 0)]
    ppermute x2, waiting for transfers between devices: 0.01 us -> 10.6 us  [padded(): after = lax.ppermute(leading, axis, down)]
    all_to_all x0 -> x1, starting transfers between devices: none -> 7.83 us  [on_device(): lax.all_to_all(jnp.stack([local_v] * lax.axis_size('seq')), 'seq', 0, 0)]
  transfers between devices with their start and end apart: 8 -> 8, of which waited for: 3 -> 5; matrix products, arithmetic and copies ran while one was open for 7% -> 9% of each run, Pallas kernels for 0% -> 0%
where the time goes in v1:
time: 623 us; the launch traced here: 620 us
  waiting for transfers between devices  227 us (36%)
  local copies, waits for them, and re-layouts  147 us (24%)
  matrix products  125 us (20%)
  blocking collectives  79.8 us (13%)
  starting transfers between devices  19 us (3%)
  between operations  14.1 us (2%)
    unnamed x5, waiting for transfers between devices  88.7 us
    psum x1, blocking collectives, on_device(): filter_gradient = lax.psum(jnp.stack(filter_rows, 0), ('dp', 'seq'))  79.8 us
    ppermute x2, waiting for transfers between devices, padded(): before = lax.ppermute(last, axis, up)  78 us
    unnamed x49, local copies, waits for them, and re-layouts  59.4 us
    all_to_all x1, waiting for transfers between devices, on_device(): lax.all_to_all(jnp.stack([local_v] * lax.axis_size('seq')), 'seq', 0, 0)  48.8 us
    dynamic_slice x24, local copies, waits for them, and re-layouts, columns(): lax.dynamic_slice_in_dim(matrix, group_index * group_width, group_width, 1)  44.6 us
    dot_general x4, matrix products, forward_group(): jnp.einsum('htu,thd->uhd', dscore, q_part, preferred_element_type=jnp.flo...  38 us
    dot_general x4, matrix products, forward_group(): jnp.einsum('htu,uhd->thd', dscore, k_part, preferred_element_type=jnp.flo...  34.2 us
  transfers between devices with their start and end apart: 8, of which 5 were waited for; matrix products, arithmetic and copies ran while one was open for 9% of the time, Pallas kernels for 0%

profile of v1, /device:TPU:1, one launch (start us, length us, event | category | flops | bytes accessed | tf_op | source)
XLA Modules:
  0.0 620.4 jit_solution(13969768179911156888)
XLA Ops:
  10.6 4.8 stack.27
  15.4 7.8 %all-to-all-start = ((bf16[16,128,2048]{1,2,0:T(8,128)(2,1)}), bf16[16,128,2048]{1,2,0:T(8,128)(2,1)}, u32[]{:S(2)}, u32[]{:S(2)}) async-start(bf16[16,128,2048]{1,2,0:T(8,128)(2,1)} %stack.27), calls=%async_computation | async-start | bytes 16777216 | tf_op jit(solution)/shard_map/all_to_all | solution.py:50
  26.2 78.0 %collective-permute-done.1 = bf16[3,2048]{1,0:T(4,128)(2,1)S(1)} collective-permute-done((bf16[3,2048]{1,0:T(4,128)(2,1)S(1)}, bf16[3,2048]{1,0:T(4,128)(2,1)S(1)}, u32[]{:S(2)}, u32[]{:S(2)}) %collective-permute-start.1) | collective-permute-done | bytes 12320 | tf_op jit(solution)/shard_map/ppermute | solution.py:18
  104.3 10.6 %collective-permute-done = bf16[3,2048]{1,0:T(4,128)(2,1)S(1)} collective-permute-done((bf16[3,2048]{1,0:T(4,128)(2,1)S(1)}, bf16[3,2048]{1,0:T(4,128)(2,1)S(1)}, u32[]{:S(2)}, u32[]{:S(2)}) %collective-permute-start) | collective-permute-done | bytes 12320 | tf_op jit(solution)/shard_map/ppermute | solution.py:19
  116.6 48.8 %all-to-all-done = bf16[16,128,2048]{1,2,0:T(8,128)(2,1)} async-done(((bf16[16,128,2048]{1,2,0:T(8,128)(2,1)}), bf16[16,128,2048]{1,2,0:T(8,128)(2,1)}, u32[]{:S(2)}, u32[]{:S(2)}) %all-to-all-start) | async-done | bytes 8388640 | tf_op jit(solution)/shard_map/all_to_all | solution.py:50
  165.4 12.3 %copy.57 = bf16[16,128,2048]{2,1,0:T(8,128)(2,1)} copy(bf16[16,128,2048]{1,2,0:T(8,128)(2,1)} %all-to-all-done) | data formatting | bytes 16777216 | tf_op jit(solution)/shard_map/all_to_all | solution.py:50
  179.0 194.3 %while.17 = (s32[]{:T(128)}, bf16[4,128,512]{1,2,0:T(8,128)(2,1)S(1)}, bf16[4,128,512]{1,2,0:T(8,128)(2,1)}, bf16[4,2048,512]{1,2,0:T(8,128)(2,1)}, bf16[4,2048,...) while((s32[]{:T(128)}, ...), condition=%wide.region_4.5_spmd.clone, body=%wide.region_0.4_spmd.clone.sunk | while | flops 1904614400 | bytes 86518528 | solution.py:97
  194.3 6.5 %fusion.111 = (f32[4,128]{1,0:T(4,128)S(1)}, f32[4,128,2048]{2,1,0:T(8,128)}) fusion(pred[128,2048]{1,0:T(8,128)(4,1)S(1)} %iota_compare_fusion.2, bf16[128,4,128]{0,2,1:T(8,128)(2,1)S(1)} %bitcast.144, bf16[2048,4,128]{0,2,1:T(8,128)(2,1)} %bitcast.126), kind=kOutput, calls=%fused_computation.95.clone.1 | convolution fusion | flops 543164416 | bytes 6686720 | tf_op jit(solution)/shard_map/while/body/eval_jaxpr/sub | solution.py:72
  200.9 8.5 %fusion.112 = bf16[4,128,128]{2,1,0:T(8,128)(2,1)S(1)} fusion(bf16[2048,4,128]{0,2,1:T(8,128)(2,1)} %bitcast.127, f32[4,128,2048]{2,1,0:T(8,128)} %fusion.110, f32[4,128,2048]{2,1,0:T(8,128)} %get-tuple-element.258, f32[4,128]{1,0:T(4,128)S(1)} %get-tuple-element.259), kind=kOutput, calls=%fused_computation.18.clone.1 | convolution fusion | flops 275843584 | bytes 10618880 | tf_op jit(solution)/shard_map/while/body/eval_jaxpr/htu,uhd->thd/dot_general | solution.py:83
  214.0 9.5 %fusion.114 = bf16[4,128,2048]{2,1,0:T(8,128)(2,1)} fusion(bf16[128,4,128]{0,2,1:T(8,128)(2,1)S(1)} %bitcast.145, f32[4,128,2048]{2,1,0:T(8,128)} %fusion.110, f32[4,128,2048]{2,1,0:T(8,128)} %get-tuple-element.258, f32[4,128]{1,0:T(4,128)S(1)} %get-tuple-element.259), kind=kOutput, calls=%fused_computation.10.clone.1 | convolution fusion | flops 275778048 | bytes 10618880 | tf_op jit(solution)/shard_map/while/body/eval_jaxpr/htu,thd->uhd/dot_general | solution.py:85
  223.5 4.1 constant_dynamic-update-slice_fusion.7
  228.9 3.2 constant_dynamic-slice_fusion.8
  243.0 6.5 %fusion.111 = (f32[4,128]{1,0:T(4,128)S(1)}, f32[4,128,2048]{2,1,0:T(8,128)}) fusion(pred[128,2048]{1,0:T(8,128)(4,1)S(1)} %iota_compare_fusion.2, bf16[128,4,128]{0,2,1:T(8,128)(2,1)S(1)} %bitcast.144, bf16[2048,4,128]{0,2,1:T(8,128)(2,1)} %bitcast.126), kind=kOutput, calls=%fused_computation.95.clone.1 | convolution fusion | flops 543164416 | bytes 6686720 | tf_op jit(solution)/shard_map/while/body/eval_jaxpr/sub | solution.py:72
  249.5 8.5 %fusion.112 = bf16[4,128,128]{2,1,0:T(8,128)(2,1)S(1)} fusion(bf16[2048,4,128]{0,2,1:T(8,128)(2,1)} %bitcast.127, f32[4,128,2048]{2,1,0:T(8,128)} %fusion.110, f32[4,128,2048]{2,1,0:T(8,128)} %get-tuple-element.258, f32[4,128]{1,0:T(4,128)S(1)} %get-tuple-element.259), kind=kOutput, calls=%fused_computation.18.clone.1 | convolution fusion | flops 275843584 | bytes 10618880 | tf_op jit(solution)/shard_map/while/body/eval_jaxpr/htu,uhd->thd/dot_general | solution.py:83
  262.7 9.5 %fusion.114 = bf16[4,128,2048]{2,1,0:T(8,128)(2,1)} fusion(bf16[128,4,128]{0,2,1:T(8,128)(2,1)S(1)} %bitcast.145, f32[4,128,2048]{2,1,0:T(8,128)} %fusion.110, f32[4,128,2048]{2,1,0:T(8,128)} %get-tuple-element.258, f32[4,128]{1,0:T(4,128)S(1)} %get-tuple-element.259), kind=kOutput, calls=%fused_computation.10.clone.1 | convolution fusion | flops 275778048 | bytes 10618880 | tf_op jit(solution)/shard_map/while/body/eval_jaxpr/htu,thd->uhd/dot_general | solution.py:85
  272.2 4.0 constant_dynamic-update-slice_fusion.7
  277.4 3.2 constant_dynamic-slice_fusion.8
  291.5 6.5 %fusion.111 = (f32[4,128]{1,0:T(4,128)S(1)}, f32[4,128,2048]{2,1,0:T(8,128)}) fusion(pred[128,2048]{1,0:T(8,128)(4,1)S(1)} %iota_compare_fusion.2, bf16[128,4,128]{0,2,1:T(8,128)(2,1)S(1)} %bitcast.144, bf16[2048,4,128]{0,2,1:T(8,128)(2,1)} %bitcast.126), kind=kOutput, calls=%fused_computation.95.clone.1 | convolution fusion | flops 543164416 | bytes 6686720 | tf_op jit(solution)/shard_map/while/body/eval_jaxpr/sub | solution.py:72
  298.0 8.5 %fusion.112 = bf16[4,128,128]{2,1,0:T(8,128)(2,1)S(1)} fusion(bf16[2048,4,128]{0,2,1:T(8,128)(2,1)} %bitcast.127, f32[4,128,2048]{2,1,0:T(8,128)} %fusion.110, f32[4,128,2048]{2,1,0:T(8,128)} %get-tuple-element.258, f32[4,128]{1,0:T(4,128)S(1)} %get-tuple-element.259), kind=kOutput, calls=%fused_computation.18.clone.1 | convolution fusion | flops 275843584 | bytes 10618880 | tf_op jit(solution)/shard_map/while/body/eval_jaxpr/htu,uhd->thd/dot_general | solution.py:83
  311.2 9.5 %fusion.114 = bf16[4,128,2048]{2,1,0:T(8,128)(2,1)} fusion(bf16[128,4,128]{0,2,1:T(8,128)(2,1)S(1)} %bitcast.145, f32[4,128,2048]{2,1,0:T(8,128)} %fusion.110, f32[4,128,2048]{2,1,0:T(8,128)} %get-tuple-element.258, f32[4,128]{1,0:T(4,128)S(1)} %get-tuple-element.259), kind=kOutput, calls=%fused_computation.10.clone.1 | convolution fusion | flops 275778048 | bytes 10618880 | tf_op jit(solution)/shard_map/while/body/eval_jaxpr/htu,thd->uhd/dot_general | solution.py:85
  320.7 4.1 constant_dynamic-update-slice_fusion.7
  340.1 6.5 %fusion.111 = (f32[4,128]{1,0:T(4,128)S(1)}, f32[4,128,2048]{2,1,0:T(8,128)}) fusion(pred[128,2048]{1,0:T(8,128)(4,1)S(1)} %iota_compare_fusion.2, bf16[128,4,128]{0,2,1:T(8,128)(2,1)S(1)} %bitcast.144, bf16[2048,4,128]{0,2,1:T(8,128)(2,1)} %bitcast.126), kind=kOutput, calls=%fused_computation.95.clone.1 | convolution fusion | flops 543164416 | bytes 6686720 | tf_op jit(solution)/shard_map/while/body/eval_jaxpr/sub | solution.py:72
  346.6 8.5 %fusion.112 = bf16[4,128,128]{2,1,0:T(8,128)(2,1)S(1)} fusion(bf16[2048,4,128]{0,2,1:T(8,128)(2,1)} %bitcast.127, f32[4,128,2048]{2,1,0:T(8,128)} %fusion.110, f32[4,128,2048]{2,1,0:T(8,128)} %get-tuple-element.258, f32[4,128]{1,0:T(4,128)S(1)} %get-tuple-element.259), kind=kOutput, calls=%fused_computation.18.clone.1 | convolution fusion | flops 275843584 | bytes 10618880 | tf_op jit(solution)/shard_map/while/body/eval_jaxpr/htu,uhd->thd/dot_general | solution.py:83
  359.8 9.5 %fusion.114 = bf16[4,128,2048]{2,1,0:T(8,128)(2,1)} fusion(bf16[128,4,128]{0,2,1:T(8,128)(2,1)S(1)} %bitcast.145, f32[4,128,2048]{2,1,0:T(8,128)} %fusion.110, f32[4,128,2048]{2,1,0:T(8,128)} %get-tuple-element.258, f32[4,128]{1,0:T(4,128)S(1)} %get-tuple-element.259), kind=kOutput, calls=%fused_computation.10.clone.1 | convolution fusion | flops 275778048 | bytes 10618880 | tf_op jit(solution)/shard_map/while/body/eval_jaxpr/htu,thd->uhd/dot_general | solution.py:85
  369.3 4.0 constant_dynamic-update-slice_fusion.7
  373.3 14.6 %copy.77 = bf16[4,2048,512]{2,0,1:T(4,128)(2,1)} copy(bf16[4,2048,512]{1,2,0:T(8,128)(2,1)} %get-tuple-element.67) | data formatting | bytes 16777216
  387.9 10.2 %copy.83 = bf16[256,8,4,512]{3,1,2,0:T(8,128)(2,1)} copy(bf16[256,8,4,512]{3,2,1,0:T(4,128)(2,1)} %bitcast.133) | data formatting | bytes 16777216
  398.1 14.5 %copy.79 = bf16[4,2048,512]{2,0,1:T(4,128)(2,1)} copy(bf16[4,2048,512]{1,2,0:T(8,128)(2,1)} %get-tuple-element.68) | data formatting | bytes 16777216
  412.7 10.2 %copy.84 = bf16[256,8,4,512]{3,1,2,0:T(8,128)(2,1)} copy(bf16[256,8,4,512]{3,2,1,0:T(4,128)(2,1)} %bitcast.134) | data formatting | bytes 16777216
  425.3 8.8 %collective-permute-start.2 = (bf16[3,2048]{1,0:T(4,128)(2,1)S(1)}, bf16[3,2048]{1,0:T(4,128)(2,1)S(1)}, u32[]{:S(2)}, u32[]{:S(2)}) collective-permute-start(bf16[3,2048]{1,0:T(4,128)(2,1)S(1)} %copy.73), channel_id=1, source_target_pairs={{0,1},{1,2},{2,3},{3,4},{4,5},{5,6},{6,7},{7,8},{8,9},{9,10},{10,1... | collective-permute-start | bytes 36872 | tf_op jit(solution)/shard_map/ppermute | solution.py:18
  437.9 79.8 %psum.7 = f32[7,2048]{1,0:T(8,128)} all-reduce(f32[7,2048]{1,0:T(8,128)S(1)} %stack.35), channel_id=1, replica_groups=mesh['dp'=16,'seq'=16] {'dp','seq'}, use_global_device_ids=true, to_apply=%region_14.15 | all-reduce | flops 14336 | bytes 114688 | tf_op jit(solution)/shard_map/psum | solution.py:118
  522.4 88.7 %reduce-scatter.9.cloned.1.call-done = bf16[128,2048]{1,0:T(8,128)(2,1)} async-done(((bf16[2048,2048]{1,0:T(8,128)(2,1)}), bf16[128,2048]{1,0:T(8,128)(2,1)}) %reduce-scatter.9.cloned.1.call-update) | async-done | bytes 524304
  (132 shorter events, 93.4 us)
Async XLA Ops:
  7.2 171.8 %all-gather.3.cloned.1.call-start = ((), (), s32[]{:S(2)}) async-start(), calls=%async_computation.3 | async-start | bytes 8912896 | tf_op jit(solution)/shard_map/all_gather | solution.py:48
  15.4 7.9 %copy-start = (bf16[1,128,2048]{2,1,0:T(8,128)(2,1)S(1)}, bf16[1,128,2048]{2,1,0:T(8,128)(2,1)}, u32[]{:S(2)}) copy-start(bf16[1,128,2048]{2,1,0:T(8,128)(2,1)} %param.10) | copy-start | bytes 1572868
  15.4 9.6 %copy-start.17 = (f32[7,2048]{1,0:T(8,128)S(1)}, f32[7,2048]{1,0:T(8,128)}, u32[]{:S(2)}) copy-start(f32[7,2048]{1,0:T(8,128)} %param.11) | copy-start | bytes 172036
  15.4 9.8 %copy-start.2 = (bf16[1,128,2048]{2,1,0:T(8,128)(2,1)S(1)}, bf16[1,128,2048]{2,1,0:T(8,128)(2,1)}, u32[]{:S(2)}) copy-start(bf16[1,128,2048]{2,1,0:T(8,128)(2,1)} %param.7) | copy-start | bytes 1572868
  15.4 150.0 %all-to-all-start = ((bf16[16,128,2048]{1,2,0:T(8,128)(2,1)}), bf16[16,128,2048]{1,2,0:T(8,128)(2,1)}, u32[]{:S(2)}, u32[]{:S(2)}) async-start(bf16[16,128,2048]{1,2,0:T(8,128)(2,1)} %stack.27), calls=%async_computation | async-start | bytes 16777216 | tf_op jit(solution)/shard_map/all_to_all | solution.py:50
  23.3 496.2 %reduce-scatter.7.cloned.1.call-start = ((), (), s32[]{:S(2)}) async-start(), calls=%async_computation.4 | async-start | bytes 8912896
  23.3 80.9 %collective-permute-start.1 = (bf16[3,2048]{1,0:T(4,128)(2,1)S(1)}, bf16[3,2048]{1,0:T(4,128)(2,1)S(1)}, u32[]{:S(2)}, u32[]{:S(2)}) collective-permute-start(bf16[3,2048]{1,0:T(4,128)(2,1)S(1)} %get-tuple-element.177), channel_id=1, source_target_pairs={{0,1},{1,2},{2,3},{3,4},{4,5},{5,6},{6,7},{7,8},{8,9},{9,10},{10,1... | collective-permute-start | bytes 36872 | tf_op jit(solution)/shard_map/ppermute | solution.py:18
  25.1 89.8 %collective-permute-start = (bf16[3,2048]{1,0:T(4,128)(2,1)S(1)}, bf16[3,2048]{1,0:T(4,128)(2,1)S(1)}, u32[]{:S(2)}, u32[]{:S(2)}) collective-permute-start(bf16[3,2048]{1,0:T(4,128)(2,1)S(1)} %get-tuple-element.176), channel_id=1, source_target_pairs={{1,0},{2,1},{3,2},{4,3},{5,4},{6,5},{7,6},{8,7},{9,8},{10,9},{11,1... | collective-permute-start | bytes 36872 | tf_op jit(solution)/shard_map/ppermute | solution.py:19
  25.1 152.6 %copy-start.3 = (f32[1,2048]{1,0:T(1,128)}, f32[1,2048]{1,0:T(1,128)S(1)}, u32[]{:S(2)}) copy-start(f32[1,2048]{1,0:T(1,128)S(1)} %get-tuple-element.178) | copy-start | bytes 24580
  25.1 152.6 %copy-start.5 = (f32[1,2048]{1,0:T(1,128)}, f32[1,2048]{1,0:T(1,128)S(1)}, u32[]{:S(2)}) copy-start(f32[1,2048]{1,0:T(1,128)S(1)} %get-tuple-element.179) | copy-start | bytes 24580
  25.1 152.6 %copy-start.7 = (f32[1,2048]{1,0:T(1,128)}, f32[1,2048]{1,0:T(1,128)S(1)}, u32[]{:S(2)}) copy-start(f32[1,2048]{1,0:T(1,128)S(1)} %get-tuple-element.180) | copy-start | bytes 24580
  25.1 152.6 %copy-start.9 = (f32[1,2048]{1,0:T(1,128)}, f32[1,2048]{1,0:T(1,128)S(1)}, u32[]{:S(2)}) copy-start(f32[1,2048]{1,0:T(1,128)S(1)} %get-tuple-element.181) | copy-start | bytes 24580
  25.2 152.6 %copy-start.11 = (f32[1,2048]{1,0:T(1,128)}, f32[1,2048]{1,0:T(1,128)S(1)}, u32[]{:S(2)}) copy-start(f32[1,2048]{1,0:T(1,128)S(1)} %get-tuple-element.182) | copy-start | bytes 24580
  25.2 152.6 %copy-start.13 = (f32[1,2048]{1,0:T(1,128)}, f32[1,2048]{1,0:T(1,128)S(1)}, u32[]{:S(2)}) copy-start(f32[1,2048]{1,0:T(1,128)S(1)} %get-tuple-element.183) | copy-start | bytes 24580
  25.2 152.6 %copy-start.15 = (f32[1,2048]{1,0:T(1,128)}, f32[1,2048]{1,0:T(1,128)S(1)}, u32[]{:S(2)}) copy-start(f32[1,2048]{1,0:T(1,128)S(1)} %get-tuple-element.184) | copy-start | bytes 24580
  209.4 3.8 copy-start.18
  258.1 3.8 copy-start.18
  306.6 3.8 copy-start.18
  355.2 3.8 copy-start.18
  398.1 212.9 %reduce-scatter.9.cloned.1.call-start = ((), (), s32[]{:S(2)}) async-start(), calls=%async_computation.5 | async-start | bytes 8912896
  422.9 1.1 copy-start.1
  424.1 93.6 %copy-start.4 = (f32[1,2048]{1,0:T(1,128)S(1)}, f32[1,2048]{1,0:T(1,128)}, u32[]{:S(2)}) copy-start(f32[1,2048]{1,0:T(1,128)} %copy-done.3) | copy-start | bytes 24580
  424.2 93.5 %copy-start.6 = (f32[1,2048]{1,0:T(1,128)S(1)}, f32[1,2048]{1,0:T(1,128)}, u32[]{:S(2)}) copy-start(f32[1,2048]{1,0:T(1,128)} %copy-done.5) | copy-start | bytes 24580
  424.2 93.5 %copy-start.8 = (f32[1,2048]{1,0:T(1,128)S(1)}, f32[1,2048]{1,0:T(1,128)}, u32[]{:S(2)}) copy-start(f32[1,2048]{1,0:T(1,128)} %copy-done.7) | copy-start | bytes 24580
  424.2 93.5 %copy-start.10 = (f32[1,2048]{1,0:T(1,128)S(1)}, f32[1,2048]{1,0:T(1,128)}, u32[]{:S(2)}) copy-start(f32[1,2048]{1,0:T(1,128)} %copy-done.9) | copy-start | bytes 24580
  424.2 93.5 %copy-start.12 = (f32[1,2048]{1,0:T(1,128)S(1)}, f32[1,2048]{1,0:T(1,128)}, u32[]{:S(2)}) copy-start(f32[1,2048]{1,0:T(1,128)} %copy-done.11) | copy-start | bytes 24580
  424.2 93.5 %copy-start.14 = (f32[1,2048]{1,0:T(1,128)S(1)}, f32[1,2048]{1,0:T(1,128)}, u32[]{:S(2)}) copy-start(f32[1,2048]{1,0:T(1,128)} %copy-done.13) | copy-start | bytes 24580
  424.2 93.5 %copy-start.16 = (f32[1,2048]{1,0:T(1,128)S(1)}, f32[1,2048]{1,0:T(1,128)}, u32[]{:S(2)}) copy-start(f32[1,2048]{1,0:T(1,128)} %copy-done.15) | copy-start | bytes 24580
  424.7 12.2 %collective-permute-start.3 = (bf16[3,2048]{1,0:T(4,128)(2,1)S(1)}, bf16[3,2048]{1,0:T(4,128)(2,1)S(1)}, u32[]{:S(2)}, u32[]{:S(2)}) collective-permute-start(bf16[3,2048]{1,0:T(4,128)(2,1)S(1)} %copy.75), channel_id=1, source_target_pairs={{1,0},{2,1},{3,2},{4,3},{5,4},{6,5},{7,6},{8,7},{9,8},{10,9},{11,1... | collective-permute-start | bytes 36872 | tf_op jit(solution)/shard_map/ppermute | solution.py:19
  425.3 11.5 %collective-permute-start.2 = (bf16[3,2048]{1,0:T(4,128)(2,1)S(1)}, bf16[3,2048]{1,0:T(4,128)(2,1)S(1)}, u32[]{:S(2)}, u32[]{:S(2)}) collective-permute-start(bf16[3,2048]{1,0:T(4,128)(2,1)S(1)} %copy.73), channel_id=1, source_target_pairs={{0,1},{1,2},{2,3},{3,4},{4,5},{5,6},{6,7},{7,8},{8,9},{9,10},{10,1... | collective-permute-start | bytes 36872 | tf_op jit(solution)/shard_map/ppermute | solution.py:18
Sparse Core Ops, SparseCore 0:
  10.3 168.6 all-gather.2
  398.2 109.7 reduce-scatter.6
  510.6 100.3 reduce-scatter.8
